TPU v7x, 256 devices: a whole 4x4x8 slice. The times are simulated.
256 devices in a mesh: gx: 8 (over x, core), yz: 32 (over z, y).
Axes of the slice: x: 4, y: 4, z: 8, core: 2. Of those that a mesh axis runs over, the one named last changes fastest.
Arguments:
- velocity: float32 [3, 256, 512, 128], P(None, 'gx', 'yz'), may hold values from -6 to 6
- old_pressure: float32 [256, 512, 128], P('gx', 'yz'), may hold values from -3 to 3
- delta_weight: bfloat16 [8, 1024, 128, 128], P('gx', 'yz'), may hold values from -0.5 to 0.5
- marker_target: float32 [8, 1024, 3, 128], P('gx', 'yz'), may hold values from -6 to 6
- pair_owner: int32 [8, 1024, 1], P('gx', 'yz'), may hold values from 0 to 31; in each aligned block of 32 rows (0 to 31, 32 to 63, ..., all dimensions but the last counted through in order) at most 4 rows name the same one
- pair_grain: int32 [8, 1024], P('gx', 'yz'), may hold values from 0 to 31
- box_anchor: int32 [8, 1024, 3], P('gx', 'yz'), may hold values from 0 to 120, as said below
Outputs:
- new_velocity: float32 [3, 256, 512, 128], P(None, 'gx', 'yz')
- pressure: float32 [256, 512, 128], P('gx', 'yz')
Inputs may be any that keep to these rules, and one draw needn't show every extreme that they name: Block r of slab i lies on tile r // 32 of that slab; its grain is owned by tile pair_owner of the same slab. Among the 32 blocks of one tile at most 4 name the same owner, and some tile reaches 4. `pair_grain`: blocks of one slab with equal owner and grain slot belong to one grain. `box_anchor`: column 0 is at most 28, column 1 at most 12, column 2 at most 120, and each of these is reached, so every box lies inside its tile.
All inputs are finite; a program needn't handle non-finite values.
Results may differ from a plain program's by a relative error of at most 0.002.
Values may be sent and summed in bfloat16 or wider, within the bound.
No kernel may reach another device: no remote copies, remote signals or barrier semaphores. Data moves between devices by JAX's collectives and lax.ppermute only.
A program may use at most 128 MiB of HBM per device.

v0:
```python
import jax
import jax.numpy as jnp
from jax import lax
from jax.sharding import PartitionSpec as P

BX = 4
BZ = 4
BY = 8
step_size = 0.1
viscosity = 1.5


def extended(block, sides, width):
    for axis, dim in sides:
        count = lax.axis_size(axis)
        forward = [(i, i + 1) for i in range(count - 1)]
        forward.append((count - 1, 0))
        backward = [(target, source) for source, target in forward]
        low = lax.ppermute(
            lax.slice_in_dim(block, block.shape[dim] - width, None, axis=dim), axis, forward
        )
        high = lax.ppermute(lax.slice_in_dim(block, 0, width, axis=dim), axis, backward)
        block = jnp.concatenate([low, block, high], axis=dim)
    return block


def inner(padded):
    return padded[..., 1:-1, 1:-1, :]


def along_x(padded):
    return 0.5 * (padded[..., 2:, 1:-1, :] - padded[..., :-2, 1:-1, :])


def along_z(padded):
    return 0.5 * (padded[..., 1:-1, 2:, :] - padded[..., 1:-1, :-2, :])


def along_y(field):
    return 0.5 * (jnp.roll(field, -1, -1) - jnp.roll(field, 1, -1))


def neighbours(padded):
    middle = inner(padded)
    total = padded[..., 2:, 1:-1, :] + padded[..., :-2, 1:-1, :]
    total = total + padded[..., 1:-1, 2:, :] + padded[..., 1:-1, :-2, :]
    return total + jnp.roll(middle, 1, -1) + jnp.roll(middle, -1, -1)


def gradient_of(padded):
    middle = inner(padded)
    return jnp.stack([along_x(padded), along_y(middle), along_z(padded)])


def predict(flow_padded):
    velocity_padded = flow_padded[:3]
    pressure_padded = flow_padded[3]
    current = inner(velocity_padded)
    laplace = neighbours(velocity_padded) - 6.0 * current
    advect = current[0] * along_x(velocity_padded)
    return current + step_size * (viscosity * laplace - advect) - gradient_of(pressure_padded)


def kernel_box_cells(anchors, box_x, box_z, box_y):
    steps_x = jnp.arange(box_x, dtype=jnp.int32)
    steps_z = jnp.arange(box_z, dtype=jnp.int32)
    steps_y = jnp.arange(box_y, dtype=jnp.int32)
    cell_x = anchors[:, 0, None, None, None] + steps_x[None, :, None, None]
    cell_z = anchors[:, 1, None, None, None] + steps_z[None, None, :, None]
    cell_y = anchors[:, 2, None, None, None] + steps_y[None, None, None, :]
    return (cell_x, cell_z, cell_y)


def walls(padded, vertical_dim):
    tile_index = lax.axis_index("yz")
    tile_total = lax.axis_size("yz")
    extent = padded.shape[vertical_dim]
    position = lax.broadcasted_iota(jnp.int32, padded.shape, vertical_dim)
    bottom_rim = jnp.logical_and(position == 0, tile_index == 0)
    top_rim = jnp.logical_and(position == extent - 1, tile_index == tile_total - 1)
    return jnp.where(jnp.logical_or(bottom_rim, top_rim), jnp.zeros((), padded.dtype), padded)


def pressure_cycle(pressure):
    padded = extended(pressure, (("gx", 0), ("yz", 1)), 1)
    return walls(padded, 1)


def body(velocity, old_pressure, delta_weight, marker_target, pair_owner, pair_grain, box_anchor):
    flow_fields = jnp.concatenate([velocity, old_pressure[None]], 0)
    flow_padded = walls(extended(flow_fields, (("gx", 1), ("yz", 2)), 1), 2)
    predicted = predict(flow_padded)
    anchors = box_anchor[0]
    owners = pair_owner[0, :, 0]
    grains = pair_grain[0]
    delta_weights = delta_weight[0]
    grain_slots = marker_target.shape[1]
    pair_total = anchors.shape[0]
    cell_x, cell_z, cell_y = kernel_box_cells(anchors, BX, BZ, BY)
    kernel_box_values = (
        predicted[:, cell_x, cell_z, cell_y].astype(jnp.bfloat16).reshape(3, pair_total, -1)
    )
    partial_force_value = jnp.einsum(
        "eky,iey->eik", delta_weights, kernel_box_values, preferred_element_type=jnp.float32
    )
    row_width = partial_force_value.shape[1] * partial_force_value.shape[2]
    flat_partial = partial_force_value.reshape(pair_total, row_width)
    targets = marker_target[0].reshape(grain_slots, row_width)
    slot_numbers = jnp.arange(grain_slots, dtype=jnp.int32)
    all_partial, all_owner, all_grain = (
        lax.all_gather(flat_partial, "yz", axis=0, tiled=True),
        lax.all_gather(owners, "yz", axis=0, tiled=True),
        lax.all_gather(grains, "yz", axis=0, tiled=True),
    )
    own_tile = lax.axis_index("yz")
    grain_keys = jnp.where(all_owner == own_tile, all_grain, grain_slots)
    select = (grain_keys[None, :] == slot_numbers[:, None]).astype(jnp.float32)
    summed = jnp.dot(
        select, all_partial, precision=lax.Precision.HIGHEST, preferred_element_type=jnp.float32
    )
    grain_force = (targets - summed).astype(jnp.bfloat16)
    all_force = lax.all_gather(grain_force, "yz", axis=0, tiled=True)
    marker_pair_force = jnp.take(all_force, owners * grain_slots + grains, axis=0)
    spread_force = jnp.einsum(
        "zwx,znw->nzx",
        delta_weights,
        marker_pair_force.reshape(pair_total, 3, -1),
        preferred_element_type=jnp.float32,
    )
    spread_force = spread_force.reshape(3, pair_total, BX, BZ, BY)
    forced_velocity = predicted + jnp.zeros_like(predicted).at[:, cell_x, cell_z, cell_y].add(
        spread_force
    )
    forced_padded = walls(extended(forced_velocity, (("gx", 1), ("yz", 2)), 1), 2)
    divergence = along_x(forced_padded[0]) + along_y(forced_velocity[1]) + along_z(forced_padded[2])
    first_padded = pressure_cycle(old_pressure)
    pressure = (neighbours(first_padded) - divergence) / 6.0
    pressure = (neighbours(pressure_cycle(pressure)) - divergence) / 6.0
    new_velocity = forced_velocity - gradient_of(pressure_cycle(pressure))
    return (new_velocity, pressure)


def solution(mesh):
    placed = (
        P(None, "gx", "yz", None),
        P("gx", "yz", None),
        P("gx", "yz", None, None),
        P("gx", "yz", None, None),
        P("gx", "yz", None),
        P("gx", "yz"),
        P("gx", "yz", None),
    )
    return jax.shard_map(
        body,
        mesh=mesh,
        in_specs=placed,
        out_specs=(P(None, "gx", "yz", None), P("gx", "yz", None)),
        check_vma=False,
    )
```

profile of v0, /device:TPU:7, one launch (start us, length us, event | category | flops | bytes accessed | tf_op | source)
XLA Modules:
  0.0 358.6 jit_solution(16332044363483749540)
XLA Ops:
  8.2 2.5 collective-permute-start
  13.3 1.9 collective-permute-done.1
  15.5 6.4 %collective-permute-start.3 = (f32[4,34,1,128]{3,0,2,1:T(4,128)S(1)}, f32[4,34,1,128]{3,0,2,1:T(4,128)S(1)}, u32[]{:S(2)}, u32[]{:S(2)}) collective-permute-start(f32[4,34,1,128]{3,0,2,1:T(4,128)S(1)} %copy.535), channel_id=1, source_target_pairs={{1,0},{2,1},{3,2},{4,3},{5,4},{6,5},{7,6},{8,7},{9,8},{10,9},{11,1... | collective-permute-start | bytes 208904 | tf_op jit(solution)/shard_map/ppermute | solution.py:22
  21.9 2.5 collective-permute-done.2
  33.1 1.5 copy_bitcast_fusion.6
  36.2 1.6 fusion.11
  37.9 17.1 %copy.528 = f32[3,32,16,128]{0,3,2,1:T(8,128)} copy(f32[3,32,16,128]{3,2,1,0:T(8,128)} %fusion.11) | data formatting | bytes 1572864
  54.9 43.8 %gather_fusion = bf16[4096,3]{1,0:T(8,128)(2,1)S(1)} fusion(f32[3,32,16,128]{0,3,2,1:T(8,128)} %copy.528, s32[4096]{0:T(1024)S(1)} %reshape.255), kind=kCustom, calls=%fused_computation | custom fusion | bytes 98304 | tf_op jit(solution)/shard_map/gather | solution.py:101
  102.8 15.8 %all-reduce.2 = (s32[1024]{0:T(1024)S(1)}, s32[1024]{0:T(1024)S(1)}) all-reduce(s32[1024]{0:T(1024)S(1)} %bitcast_dynamic-update-slice_fusion.1, s32[1024]{0:T(1024)S(1)} %bitcast_dynamic-update-slice_fusion), channel_id=3, replica_groups=mesh['gx'=8,'yz'=32] {'yz'}, use_global_device_ids=true, to_apply=%add.1 | all-reduce | flops 2048 | bytes 16384 | tf_op jit(solution)/shard_map/all_gather | solution.py:113
  120.1 3.9 %collective-permute-start.7 = (f32[34,1,128]{2,0,1:T(8,128)S(1)}, f32[34,1,128]{2,0,1:T(8,128)S(1)}, u32[]{:S(2)}, u32[]{:S(2)}) collective-permute-start(f32[34,1,128]{2,0,1:T(8,128)S(1)} %get-tuple-element.71), channel_id=1, source_target_pairs={{1,0},{2,1},{3,2},{4,3},{5,4},{6,5},{7,6},{8,7},{9,8},{10,9},{11,1... | collective-permute-start | bytes 52232 | tf_op jit(solution)/shard_map/ppermute | solution.py:22
  126.3 45.6 %all-gather.4.cloned.1.call-done = f32[1024,384]{1,0:T(8,128)} async-done(((f32[32,384]{1,0:T(8,128)}), f32[1024,384]{1,0:T(8,128)}) %all-gather.4.cloned.1.call-update) | async-done | bytes 1572880 | tf_op jit(solution)/shard_map/all_gather | solution.py:111
  171.9 2.1 fusion
  174.0 36.3 %all_gather.15 = bf16[1024,384]{1,0:T(8,128)(2,1)S(1)} all-gather(bf16[32,384]{1,0:T(8,128)(2,1)S(1)} %fusion), channel_id=1, replica_groups=mesh['gx'=8,'yz'=32] {'yz'}, dimensions={0}, use_global_device_ids=true | all-gather | bytes 811008 | tf_op jit(solution)/shard_map/all_gather | solution.py:122
  211.3 2.0 copy.532
  213.3 42.0 %scatter_fusion = f32[3,65536]{0,1:T(8,128)} fusion(f32[3,65536]{0,1:T(8,128)} %bitcast.96, s32[4096]{0:T(1024)S(1)} %reshape.269, f32[4096,3]{1,0:T(8,128)} %bitcast.106), kind=kCustom, calls=%fused_computation.2 | custom fusion | flops 12288 | bytes 163840
  255.3 20.3 %slice_reduce_fusion = f32[65536]{0:T(1024)S(1)} fusion(f32[3,65536]{0,1:T(8,128)} %scatter_fusion), kind=kLoop, calls=%fused_computation.3 | loop fusion | bytes 524288 | tf_op jit(solution)/shard_map/slice | solution.py:135
  275.6 18.8 %copy.526 = f32[3,32,16,128]{3,2,1,0:T(8,128)S(1)} copy(f32[3,32,16,128]{0,3,2,1:T(8,128)} %bitcast.97) | data formatting | bytes 1572864 | tf_op jit(solution)/shard_map/scatter-add | solution.py:131
  294.4 17.8 %collective-permute-start.8 = (f32[3,1,16,128]{3,2,1,0:T(8,128)S(1)}, f32[3,1,16,128]{3,2,1,0:T(8,128)S(1)}, u32[]{:S(2)}, u32[]{:S(2)}) collective-permute-start(f32[3,1,16,128]{3,2,1,0:T(8,128)S(1)} %get-tuple-element.48), channel_id=1, source_target_pairs={{0,32},{32,64},{64,96},{96,128},{128,160},{160,192},{192,224},{224... | collective-permute-start | bytes 73736 | tf_op jit(solution)/shard_map/ppermute | solution.py:19
  313.2 3.5 collective-permute-done.9
  316.9 4.8 %collective-permute-start.11 = (f32[3,34,1,128]{3,2,1,0:T(1,128)S(1)}, f32[3,34,1,128]{3,2,1,0:T(1,128)S(1)}, u32[]{:S(2)}, u32[]{:S(2)}) collective-permute-start(f32[3,34,1,128]{3,2,1,0:T(1,128)S(1)} %get-tuple-element.47), channel_id=1, source_target_pairs={{1,0},{2,1},{3,2},{4,3},{5,4},{6,5},{7,6},{8,7},{9,8},{10,9},{11,1... | collective-permute-start | bytes 156680 | tf_op jit(solution)/shard_map/ppermute | solution.py:22
  326.7 3.5 collective-permute-done.13
  330.3 5.1 %collective-permute-start.15 = (f32[34,1,128]{2,0,1:T(8,128)S(1)}, f32[34,1,128]{2,0,1:T(8,128)S(1)}, u32[]{:S(2)}, u32[]{:S(2)}) collective-permute-start(f32[34,1,128]{2,0,1:T(8,128)S(1)} %get-tuple-element.69), channel_id=1, source_target_pairs={{1,0},{2,1},{3,2},{4,3},{5,4},{6,5},{7,6},{8,7},{9,8},{10,9},{11,1... | collective-permute-start | bytes 52232 | tf_op jit(solution)/shard_map/ppermute | solution.py:22
  338.9 3.5 collective-permute-done.17
  342.5 5.2 %collective-permute-start.19 = (f32[34,1,128]{2,0,1:T(8,128)S(1)}, f32[34,1,128]{2,0,1:T(8,128)S(1)}, u32[]{:S(2)}, u32[]{:S(2)}) collective-permute-start(f32[34,1,128]{2,0,1:T(8,128)S(1)} %get-tuple-element.67), channel_id=1, source_target_pairs={{1,0},{2,1},{3,2},{4,3},{5,4},{6,5},{7,6},{8,7},{9,8},{10,9},{11,1... | collective-permute-start | bytes 52232 | tf_op jit(solution)/shard_map/ppermute | solution.py:22
  (174 shorter events, 35.8 us)
Async XLA Ops:
  7.2 91.7 %copy-start = (bf16[1,32,128,128]{3,2,1,0:T(8,128)(2,1)S(1)}, bf16[1,32,128,128]{3,2,1,0:T(8,128)(2,1)}, u32[]{:S(2)}) copy-start(bf16[1,32,128,128]{3,2,1,0:T(8,128)(2,1)} %param.9) | copy-start | bytes 3145732
  7.2 164.7 %all-gather.4.cloned.1.call-start = ((), (), s32[]{:S(2)}) async-start(), calls=%async_computation | async-start | bytes 1622016 | tf_op jit(solution)/shard_map/all_gather | solution.py:111
  8.2 5.1 %collective-permute-start = (f32[4,1,16,128]{3,2,1,0:T(8,128)S(1)}, f32[4,1,16,128]{3,2,1,0:T(8,128)S(1)}, u32[]{:S(2)}, u32[]{:S(2)}) collective-permute-start(f32[4,1,16,128]{3,2,1,0:T(8,128)S(1)} %get-tuple-element.44), channel_id=1, source_target_pairs={{0,32},{32,64},{64,96},{96,128},{128,160},{160,192},{192,224},{224... | collective-permute-start | bytes 98312 | tf_op jit(solution)/shard_map/ppermute | solution.py:19
  10.6 4.6 %collective-permute-start.1 = (f32[4,1,16,128]{3,2,1,0:T(8,128)S(1)}, f32[4,1,16,128]{3,2,1,0:T(8,128)S(1)}, u32[]{:S(2)}, u32[]{:S(2)}) collective-permute-start(f32[4,1,16,128]{3,2,1,0:T(8,128)S(1)} %get-tuple-element.45), channel_id=1, source_target_pairs={{32,0},{64,32},{96,64},{128,96},{160,128},{192,160},{224,192},{0,2... | collective-permute-start | bytes 98312 | tf_op jit(solution)/shard_map/ppermute | solution.py:22
  15.3 9.0 %collective-permute-start.2 = (f32[4,34,1,128]{3,0,2,1:T(4,128)S(1)}, f32[4,34,1,128]{3,0,2,1:T(4,128)S(1)}, u32[]{:S(2)}, u32[]{:S(2)}) collective-permute-start(f32[4,34,1,128]{3,0,2,1:T(4,128)S(1)} %copy.534), channel_id=1, source_target_pairs={{0,1},{1,2},{2,3},{3,4},{4,5},{5,6},{6,7},{7,8},{8,9},{9,10},{10,1... | collective-permute-start | bytes 208904 | tf_op jit(solution)/shard_map/ppermute | solution.py:19
  15.5 9.0 %collective-permute-start.3 = (f32[4,34,1,128]{3,0,2,1:T(4,128)S(1)}, f32[4,34,1,128]{3,0,2,1:T(4,128)S(1)}, u32[]{:S(2)}, u32[]{:S(2)}) collective-permute-start(f32[4,34,1,128]{3,0,2,1:T(4,128)S(1)} %copy.535), channel_id=1, source_target_pairs={{1,0},{2,1},{3,2},{4,3},{5,4},{6,5},{7,6},{8,7},{9,8},{10,9},{11,1... | collective-permute-start | bytes 208904 | tf_op jit(solution)/shard_map/ppermute | solution.py:22
  98.8 25.2 %copy-start.14 = (f32[1,32,3,128]{3,1,2,0:T(8,128)S(1)}, f32[1,32,3,128]{3,1,2,0:T(8,128)}, u32[]{:S(2)}) copy-start(f32[1,32,3,128]{3,1,2,0:T(8,128)} %param.10) | copy-start | bytes 147460
  99.5 25.7 %copy-start.17 = (pred[18]{0:T(512)(128)(4,1)S(1)}, pred[18]{0:T(512)(128)(4,1)}, u32[]{:S(2)}) copy-start(pred[18]{0:T(512)(128)(4,1)} %copy-done.16) | copy-start | bytes 58
  100.2 18.9 %collective-permute-start.4 = (f32[1,16,128]{2,0,1:T(1,128)S(1)}, f32[1,16,128]{2,0,1:T(1,128)S(1)}, u32[]{:S(2)}, u32[]{:S(2)}) collective-permute-start(f32[1,16,128]{2,0,1:T(1,128)S(1)} %bitcast.120), channel_id=1, source_target_pairs={{0,32},{32,64},{64,96},{96,128},{128,160},{160,192},{192,224},{224... | collective-permute-start | bytes 24584 | tf_op jit(solution)/shard_map/ppermute | solution.py:19
  101.4 17.7 %collective-permute-start.5 = (f32[1,16,128]{2,0,1:T(1,128)S(1)}, f32[1,16,128]{2,0,1:T(1,128)S(1)}, u32[]{:S(2)}, u32[]{:S(2)}) collective-permute-start(f32[1,16,128]{2,0,1:T(1,128)S(1)} %bitcast.119), channel_id=1, source_target_pairs={{32,0},{64,32},{96,64},{128,96},{160,128},{192,160},{224,192},{0,2... | collective-permute-start | bytes 24584 | tf_op jit(solution)/shard_map/ppermute | solution.py:22
  119.1 6.1 %collective-permute-start.6 = (f32[34,1,128]{2,0,1:T(8,128)S(1)}, f32[34,1,128]{2,0,1:T(8,128)S(1)}, u32[]{:S(2)}, u32[]{:S(2)}) collective-permute-start(f32[34,1,128]{2,0,1:T(8,128)S(1)} %get-tuple-element.70), channel_id=1, source_target_pairs={{0,1},{1,2},{2,3},{3,4},{4,5},{5,6},{6,7},{7,8},{8,9},{9,10},{10,1... | collective-permute-start | bytes 52232 | tf_op jit(solution)/shard_map/ppermute | solution.py:19
  120.1 5.1 %collective-permute-start.7 = (f32[34,1,128]{2,0,1:T(8,128)S(1)}, f32[34,1,128]{2,0,1:T(8,128)S(1)}, u32[]{:S(2)}, u32[]{:S(2)}) collective-permute-start(f32[34,1,128]{2,0,1:T(8,128)S(1)} %get-tuple-element.71), channel_id=1, source_target_pairs={{1,0},{2,1},{3,2},{4,3},{5,4},{6,5},{7,6},{8,7},{9,8},{10,9},{11,1... | collective-permute-start | bytes 52232 | tf_op jit(solution)/shard_map/ppermute | solution.py:22
  294.4 18.8 %collective-permute-start.8 = (f32[3,1,16,128]{3,2,1,0:T(8,128)S(1)}, f32[3,1,16,128]{3,2,1,0:T(8,128)S(1)}, u32[]{:S(2)}, u32[]{:S(2)}) collective-permute-start(f32[3,1,16,128]{3,2,1,0:T(8,128)S(1)} %get-tuple-element.48), channel_id=1, source_target_pairs={{0,32},{32,64},{64,96},{96,128},{128,160},{160,192},{192,224},{224... | collective-permute-start | bytes 73736 | tf_op jit(solution)/shard_map/ppermute | solution.py:19
  312.2 4.5 %collective-permute-start.9 = (f32[3,1,16,128]{3,2,1,0:T(8,128)S(1)}, f32[3,1,16,128]{3,2,1,0:T(8,128)S(1)}, u32[]{:S(2)}, u32[]{:S(2)}) collective-permute-start(f32[3,1,16,128]{3,2,1,0:T(8,128)S(1)} %get-tuple-element.49), channel_id=1, source_target_pairs={{32,0},{64,32},{96,64},{128,96},{160,128},{192,160},{224,192},{0,2... | collective-permute-start | bytes 73736 | tf_op jit(solution)/shard_map/ppermute | solution.py:22
  316.8 6.4 %collective-permute-start.10 = (f32[3,34,1,128]{3,2,1,0:T(1,128)S(1)}, f32[3,34,1,128]{3,2,1,0:T(1,128)S(1)}, u32[]{:S(2)}, u32[]{:S(2)}) collective-permute-start(f32[3,34,1,128]{3,2,1,0:T(1,128)S(1)} %get-tuple-element.46), channel_id=1, source_target_pairs={{0,1},{1,2},{2,3},{3,4},{4,5},{5,6},{6,7},{7,8},{8,9},{9,10},{10,1... | collective-permute-start | bytes 156680 | tf_op jit(solution)/shard_map/ppermute | solution.py:19
  316.9 6.3 %collective-permute-start.11 = (f32[3,34,1,128]{3,2,1,0:T(1,128)S(1)}, f32[3,34,1,128]{3,2,1,0:T(1,128)S(1)}, u32[]{:S(2)}, u32[]{:S(2)}) collective-permute-start(f32[3,34,1,128]{3,2,1,0:T(1,128)S(1)} %get-tuple-element.47), channel_id=1, source_target_pairs={{1,0},{2,1},{3,2},{4,3},{5,4},{6,5},{7,6},{8,7},{9,8},{10,9},{11,1... | collective-permute-start | bytes 156680 | tf_op jit(solution)/shard_map/ppermute | solution.py:22
  324.8 2.0 collective-permute-start.12
  325.9 4.3 %collective-permute-start.13 = (f32[1,16,128]{2,0,1:T(1,128)S(1)}, f32[1,16,128]{2,0,1:T(1,128)S(1)}, u32[]{:S(2)}, u32[]{:S(2)}) collective-permute-start(f32[1,16,128]{2,0,1:T(1,128)S(1)} %get-tuple-element.75), channel_id=1, source_target_pairs={{32,0},{64,32},{96,64},{128,96},{160,128},{192,160},{224,192},{0,2... | collective-permute-start | bytes 24584 | tf_op jit(solution)/shard_map/ppermute | solution.py:22
  330.2 6.3 %collective-permute-start.14 = (f32[34,1,128]{2,0,1:T(8,128)S(1)}, f32[34,1,128]{2,0,1:T(8,128)S(1)}, u32[]{:S(2)}, u32[]{:S(2)}) collective-permute-start(f32[34,1,128]{2,0,1:T(8,128)S(1)} %get-tuple-element.68), channel_id=1, source_target_pairs={{0,1},{1,2},{2,3},{3,4},{4,5},{5,6},{6,7},{7,8},{8,9},{9,10},{10,1... | collective-permute-start | bytes 52232 | tf_op jit(solution)/shard_map/ppermute | solution.py:19
  330.3 6.2 %collective-permute-start.15 = (f32[34,1,128]{2,0,1:T(8,128)S(1)}, f32[34,1,128]{2,0,1:T(8,128)S(1)}, u32[]{:S(2)}, u32[]{:S(2)}) collective-permute-start(f32[34,1,128]{2,0,1:T(8,128)S(1)} %get-tuple-element.69), channel_id=1, source_target_pairs={{1,0},{2,1},{3,2},{4,3},{5,4},{6,5},{7,6},{8,7},{9,8},{10,9},{11,1... | collective-permute-start | bytes 52232 | tf_op jit(solution)/shard_map/ppermute | solution.py:22
  337.2 1.7 collective-permute-start.16
  338.1 4.3 %collective-permute-start.17 = (f32[1,16,128]{2,0,1:T(1,128)S(1)}, f32[1,16,128]{2,0,1:T(1,128)S(1)}, u32[]{:S(2)}, u32[]{:S(2)}) collective-permute-start(f32[1,16,128]{2,0,1:T(1,128)S(1)} %get-tuple-element.73), channel_id=1, source_target_pairs={{32,0},{64,32},{96,64},{128,96},{160,128},{192,160},{224,192},{0,2... | collective-permute-start | bytes 24584 | tf_op jit(solution)/shard_map/ppermute | solution.py:22
  342.4 6.4 %collective-permute-start.18 = (f32[34,1,128]{2,0,1:T(8,128)S(1)}, f32[34,1,128]{2,0,1:T(8,128)S(1)}, u32[]{:S(2)}, u32[]{:S(2)}) collective-permute-start(f32[34,1,128]{2,0,1:T(8,128)S(1)} %get-tuple-element.66), channel_id=1, source_target_pairs={{0,1},{1,2},{2,3},{3,4},{4,5},{5,6},{6,7},{7,8},{8,9},{9,10},{10,1... | collective-permute-start | bytes 52232 | tf_op jit(solution)/shard_map/ppermute | solution.py:19
  342.5 6.3 %collective-permute-start.19 = (f32[34,1,128]{2,0,1:T(8,128)S(1)}, f32[34,1,128]{2,0,1:T(8,128)S(1)}, u32[]{:S(2)}, u32[]{:S(2)}) collective-permute-start(f32[34,1,128]{2,0,1:T(8,128)S(1)} %get-tuple-element.67), channel_id=1, source_target_pairs={{1,0},{2,1},{3,2},{4,3},{5,4},{6,5},{7,6},{8,7},{9,8},{10,9},{11,1... | collective-permute-start | bytes 52232 | tf_op jit(solution)/shard_map/ppermute | solution.py:22
  (22 other events, 162.0 us)
Sparse Core Ops, SparseCore 0:
  100.3 71.5 all-gather.3
where the time goes:
time: 360 us; the launch traced here: 359 us
  local copies, waits for them, and re-layouts  120 us (33%)
  waiting for transfers between devices  65.7 us (18%)
  blocking collectives  52.1 us (14%)
  other arithmetic  51.9 us (14%)
  starting transfers between devices  50.3 us (14%)
  between operations  15.5 us (4%)
    all_gather x1, waiting for transfers between devices, body(): lax.all_gather(flat_partial, 'yz', axis=0, tiled=True)  45.6 us
    gather x1, local copies, waits for them, and re-layouts, body(): predicted[:, cell_x, cell_z, cell_y].astype(jnp.bfloat16)  43.8 us
    unnamed x4, other arithmetic  42.2 us
    all_gather x1, blocking collectives, body(): all_force = lax.all_gather(grain_force, 'yz', axis=0, tiled=True)  36.3 us
    ppermute x10, starting transfers between devices, extended(): lax.ppermute(lax.slice_in_dim(block, 0, width, axis=dim), axis, backward)  25.4 us
    ppermute x10, starting transfers between devices, extended(): lax.ppermute(lax.slice_in_dim(block, block.shape[dim] - width, None, axis...  24.9 us
    unnamed x69, local copies, waits for them, and re-layouts  22 us
    slice x1, local copies, waits for them, and re-layouts, body(): forced_velocity[1]  20.3 us
  transfers between devices with their start and end apart: 21, of which 13 were waited for; matrix products, arithmetic and copies ran while one was open for 2% of the time, Pallas kernels for 0%

commit v1 on v0

--- a/solution.py
+++ b/solution.py
@@ -87,6 +87,12 @@
 
 
 def body(velocity, old_pressure, delta_weight, marker_target, pair_owner, pair_grain, box_anchor):
+
+    def state_search(message):
+        axis_id = "yz"
+        arr_next = jnp.concatenate(tuple((message for _ in range(jax.lax.axis_size(axis_id)))), 0)
+        return jax.lax.all_to_all(arr_next, axis_id, 0, 0, tiled=True)
+
     flow_fields = jnp.concatenate([velocity, old_pressure[None]], 0)
     flow_padded = walls(extended(flow_fields, (("gx", 1), ("yz", 2)), 1), 2)
     predicted = predict(flow_padded)
@@ -110,7 +116,7 @@
     all_partial, all_owner, all_grain = (
         lax.all_gather(flat_partial, "yz", axis=0, tiled=True),
         lax.all_gather(owners, "yz", axis=0, tiled=True),
-        lax.all_gather(grains, "yz", axis=0, tiled=True),
+        state_search(grains),
     )
     own_tile = lax.axis_index("yz")
     grain_keys = jnp.where(all_owner == own_tile, all_grain, grain_slots)

time: 360 us -> 360 us (level)
  waiting for transfers between devices: 65.7 us -> 54.9 us
  starting transfers between devices: 50.3 us -> 58.6 us
    unnamed x0 -> x1, blocking collectives: none -> 16.3 us
    all_gather x1 -> x0, blocking collectives: 15.8 us -> none  [body(): lax.all_gather(grains, 'yz', axis=0, tiled=True)]
    all_gather x1, waiting for transfers between devices: 45.6 us -> 34.3 us  [body(): lax.all_gather(flat_partial, 'yz', axis=0, tiled=True)]
    all_to_all x0 -> x1, starting transfers between devices: none -> 7.21 us  [state_search(): return jax.lax.all_to_all(arr_next, axis_id, 0, 0, tiled=True)]
    unnamed x69 -> x67, local copies, waits for them, and re-layouts: 22 us -> 22 us
  transfers between devices with their start and end apart: 21 -> 22, of which waited for: 13 -> 13; matrix products, arithmetic and copies ran while one was open for 2% -> 2% of each run, Pallas kernels for 0% -> 0%
where the time goes in v1:
time: 360 us; the launch traced here: 359 us
  local copies, waits for them, and re-layouts  122 us (34%)
  starting transfers between devices  58.6 us (16%)
  waiting for transfers between devices  54.9 us (15%)
  other arithmetic  52.6 us (15%)
  blocking collectives  52.6 us (15%)
  between operations  15.5 us (4%)
    gather x1, local copies, waits for them, and re-layouts, body(): predicted[:, cell_x, cell_z, cell_y].astype(jnp.bfloat16)  44 us
    unnamed x4, other arithmetic  42.2 us
    all_gather x1, blocking collectives, body(): all_force = lax.all_gather(grain_force, 'yz', axis=0, tiled=True)  36.3 us
    all_gather x1, waiting for transfers between devices, body(): lax.all_gather(flat_partial, 'yz', axis=0, tiled=True)  34.3 us
    ppermute x10, starting transfers between devices, extended(): lax.ppermute(lax.slice_in_dim(block, block.shape[dim] - width, None, axis...  26 us
    ppermute x10, starting transfers between devices, extended(): lax.ppermute(lax.slice_in_dim(block, 0, width, axis=dim), axis, backward)  25.3 us
    unnamed x67, local copies, waits for them, and re-layouts  22 us
    slice x1, local copies, waits for them, and re-layouts, body(): forced_velocity[1]  20.3 us
  transfers between devices with their start and end apart: 22, of which 13 were waited for; matrix products, arithmetic and copies ran while one was open for 2% of the time, Pallas kernels for 0%

profile of v1, /device:TPU:7, one launch (start us, length us, event | category | flops | bytes accessed | tf_op | source)
XLA Modules:
  0.0 358.8 jit_solution(5711455390793578712)
XLA Ops:
  8.2 2.5 collective-permute-start
  13.3 1.9 collective-permute-done.1
  15.5 6.4 %collective-permute-start.3 = (f32[4,34,1,128]{3,0,2,1:T(4,128)S(1)}, f32[4,34,1,128]{3,0,2,1:T(4,128)S(1)}, u32[]{:S(2)}, u32[]{:S(2)}) collective-permute-start(f32[4,34,1,128]{3,0,2,1:T(4,128)S(1)} %copy.535), channel_id=1, source_target_pairs={{1,0},{2,1},{3,2},{4,3},{5,4},{6,5},{7,6},{8,7},{9,8},{10,9},{11,1... | collective-permute-start | bytes 208904 | tf_op jit(solution)/shard_map/ppermute | solution.py:22
  21.9 2.5 collective-permute-done.2
  37.9 17.2 %copy.528 = f32[3,32,16,128]{0,3,2,1:T(8,128)} copy(f32[3,32,16,128]{3,2,1,0:T(8,128)} %fusion.11) | data formatting | bytes 1572864
  55.1 44.0 %gather_fusion = bf16[4096,3]{1,0:T(8,128)(2,1)S(1)} fusion(f32[3,32,16,128]{0,3,2,1:T(8,128)} %copy.528, s32[4096]{0:T(1024)S(1)} %reshape.325), kind=kCustom, calls=%fused_computation | custom fusion | bytes 98304 | tf_op jit(solution)/shard_map/gather | solution.py:107
  101.2 7.2 %all-to-all-start = ((s32[32,32,1]{1,2,0:T(1,128)}), s32[32,32,1]{1,2,0:T(1,128)S(1)}, u32[]{:S(2)}, u32[]{:S(2)}) async-start(s32[32,32,1]{1,2,0:T(1,128)} %concatenate.137), calls=%async_computation | async-start | bytes 32768 | tf_op jit(solution)/shard_map/all_to_all | solution.py:94
  108.5 2.2 collective-permute-start.4
  113.0 16.3 %all-reduce = s32[1024]{0:T(1024)S(1)} all-reduce(s32[1024]{0:T(1024)S(1)} %bitcast_dynamic-update-slice_fusion), channel_id=2, replica_groups=mesh['gx'=8,'yz'=32] {'yz'}, use_global_device_ids=true, to_apply=%add | all-reduce | flops 1024 | bytes 8192
  131.7 3.8 %collective-permute-start.7 = (f32[34,1,128]{2,0,1:T(8,128)S(1)}, f32[34,1,128]{2,0,1:T(8,128)S(1)}, u32[]{:S(2)}, u32[]{:S(2)}) collective-permute-start(f32[34,1,128]{2,0,1:T(8,128)S(1)} %get-tuple-element.69), channel_id=1, source_target_pairs={{1,0},{2,1},{3,2},{4,3},{5,4},{6,5},{7,6},{8,7},{9,8},{10,9},{11,1... | collective-permute-start | bytes 52232 | tf_op jit(solution)/shard_map/ppermute | solution.py:22
  137.8 34.3 %all-gather.3.cloned.1.call-done = f32[1024,384]{1,0:T(8,128)} async-done(((f32[32,384]{1,0:T(8,128)}), f32[1024,384]{1,0:T(8,128)}) %all-gather.3.cloned.1.call-update) | async-done | bytes 1572880 | tf_op jit(solution)/shard_map/all_gather | solution.py:117
  172.1 2.1 fusion
  174.2 36.3 %all_gather.11 = bf16[1024,384]{1,0:T(8,128)(2,1)S(1)} all-gather(bf16[32,384]{1,0:T(8,128)(2,1)S(1)} %fusion), channel_id=1, replica_groups=mesh['gx'=8,'yz'=32] {'yz'}, dimensions={0}, use_global_device_ids=true | all-gather | bytes 811008 | tf_op jit(solution)/shard_map/all_gather | solution.py:128
  211.5 2.0 copy.532
  213.5 42.0 %scatter_fusion = f32[3,65536]{0,1:T(8,128)} fusion(f32[3,65536]{0,1:T(8,128)} %bitcast.96, s32[4096]{0:T(1024)S(1)} %reshape.339, f32[4096,3]{1,0:T(8,128)} %bitcast.106), kind=kCustom, calls=%fused_computation.2 | custom fusion | flops 12288 | bytes 163840
  255.5 20.3 %slice_reduce_fusion = f32[65536]{0:T(1024)S(1)} fusion(f32[3,65536]{0,1:T(8,128)} %scatter_fusion), kind=kLoop, calls=%fused_computation.3 | loop fusion | bytes 524288 | tf_op jit(solution)/shard_map/slice | solution.py:141
  275.8 18.8 %copy.526 = f32[3,32,16,128]{3,2,1,0:T(8,128)S(1)} copy(f32[3,32,16,128]{0,3,2,1:T(8,128)} %bitcast.97) | data formatting | bytes 1572864 | tf_op jit(solution)/shard_map/scatter-add | solution.py:137
  294.6 17.8 %collective-permute-start.8 = (f32[3,1,16,128]{3,2,1,0:T(8,128)S(1)}, f32[3,1,16,128]{3,2,1,0:T(8,128)S(1)}, u32[]{:S(2)}, u32[]{:S(2)}) collective-permute-start(f32[3,1,16,128]{3,2,1,0:T(8,128)S(1)} %get-tuple-element.46), channel_id=1, source_target_pairs={{0,32},{32,64},{64,96},{96,128},{128,160},{160,192},{192,224},{224... | collective-permute-start | bytes 73736 | tf_op jit(solution)/shard_map/ppermute | solution.py:19
  313.4 3.5 collective-permute-done.9
  317.1 4.8 %collective-permute-start.11 = (f32[3,34,1,128]{3,2,1,0:T(1,128)S(1)}, f32[3,34,1,128]{3,2,1,0:T(1,128)S(1)}, u32[]{:S(2)}, u32[]{:S(2)}) collective-permute-start(f32[3,34,1,128]{3,2,1,0:T(1,128)S(1)} %get-tuple-element.45), channel_id=1, source_target_pairs={{1,0},{2,1},{3,2},{4,3},{5,4},{6,5},{7,6},{8,7},{9,8},{10,9},{11,1... | collective-permute-start | bytes 156680 | tf_op jit(solution)/shard_map/ppermute | solution.py:22
  326.9 3.5 collective-permute-done.13
  330.5 5.1 %collective-permute-start.15 = (f32[34,1,128]{2,0,1:T(8,128)S(1)}, f32[34,1,128]{2,0,1:T(8,128)S(1)}, u32[]{:S(2)}, u32[]{:S(2)}) collective-permute-start(f32[34,1,128]{2,0,1:T(8,128)S(1)} %get-tuple-element.67), channel_id=1, source_target_pairs={{1,0},{2,1},{3,2},{4,3},{5,4},{6,5},{7,6},{8,7},{9,8},{10,9},{11,1... | collective-permute-start | bytes 52232 | tf_op jit(solution)/shard_map/ppermute | solution.py:22
  339.1 3.5 collective-permute-done.17
  342.7 5.2 %collective-permute-start.19 = (f32[34,1,128]{2,0,1:T(8,128)S(1)}, f32[34,1,128]{2,0,1:T(8,128)S(1)}, u32[]{:S(2)}, u32[]{:S(2)}) collective-permute-start(f32[34,1,128]{2,0,1:T(8,128)S(1)} %get-tuple-element.65), channel_id=1, source_target_pairs={{1,0},{2,1},{3,2},{4,3},{5,4},{6,5},{7,6},{8,7},{9,8},{10,9},{11,1... | collective-permute-start | bytes 52232 | tf_op jit(solution)/shard_map/ppermute | solution.py:22
  (178 shorter events, 40.2 us)
Async XLA Ops:
  7.2 92.1 %copy-start = (bf16[1,32,128,128]{3,2,1,0:T(8,128)(2,1)S(1)}, bf16[1,32,128,128]{3,2,1,0:T(8,128)(2,1)}, u32[]{:S(2)}) copy-start(bf16[1,32,128,128]{3,2,1,0:T(8,128)(2,1)} %param.9) | copy-start | bytes 3145732
  7.2 164.9 %all-gather.3.cloned.1.call-start = ((), (), s32[]{:S(2)}) async-start(), calls=%async_computation.1 | async-start | bytes 1622016 | tf_op jit(solution)/shard_map/all_gather | solution.py:117
  8.2 5.1 %collective-permute-start = (f32[4,1,16,128]{3,2,1,0:T(8,128)S(1)}, f32[4,1,16,128]{3,2,1,0:T(8,128)S(1)}, u32[]{:S(2)}, u32[]{:S(2)}) collective-permute-start(f32[4,1,16,128]{3,2,1,0:T(8,128)S(1)} %get-tuple-element.42), channel_id=1, source_target_pairs={{0,32},{32,64},{64,96},{96,128},{128,160},{160,192},{192,224},{224... | collective-permute-start | bytes 98312 | tf_op jit(solution)/shard_map/ppermute | solution.py:19
  10.6 4.6 %collective-permute-start.1 = (f32[4,1,16,128]{3,2,1,0:T(8,128)S(1)}, f32[4,1,16,128]{3,2,1,0:T(8,128)S(1)}, u32[]{:S(2)}, u32[]{:S(2)}) collective-permute-start(f32[4,1,16,128]{3,2,1,0:T(8,128)S(1)} %get-tuple-element.43), channel_id=1, source_target_pairs={{32,0},{64,32},{96,64},{128,96},{160,128},{192,160},{224,192},{0,2... | collective-permute-start | bytes 98312 | tf_op jit(solution)/shard_map/ppermute | solution.py:22
  15.3 9.0 %collective-permute-start.2 = (f32[4,34,1,128]{3,0,2,1:T(4,128)S(1)}, f32[4,34,1,128]{3,0,2,1:T(4,128)S(1)}, u32[]{:S(2)}, u32[]{:S(2)}) collective-permute-start(f32[4,34,1,128]{3,0,2,1:T(4,128)S(1)} %copy.534), channel_id=1, source_target_pairs={{0,1},{1,2},{2,3},{3,4},{4,5},{5,6},{6,7},{7,8},{8,9},{9,10},{10,1... | collective-permute-start | bytes 208904 | tf_op jit(solution)/shard_map/ppermute | solution.py:19
  15.5 9.0 %collective-permute-start.3 = (f32[4,34,1,128]{3,0,2,1:T(4,128)S(1)}, f32[4,34,1,128]{3,0,2,1:T(4,128)S(1)}, u32[]{:S(2)}, u32[]{:S(2)}) collective-permute-start(f32[4,34,1,128]{3,0,2,1:T(4,128)S(1)} %copy.535), channel_id=1, source_target_pairs={{1,0},{2,1},{3,2},{4,3},{5,4},{6,5},{7,6},{8,7},{9,8},{10,9},{11,1... | collective-permute-start | bytes 208904 | tf_op jit(solution)/shard_map/ppermute | solution.py:22
  99.9 36.8 %copy-start.17 = (pred[18]{0:T(512)(128)(4,1)S(1)}, pred[18]{0:T(512)(128)(4,1)}, u32[]{:S(2)}) copy-start(pred[18]{0:T(512)(128)(4,1)} %copy-done.16) | copy-start | bytes 58
  101.2 28.1 %all-to-all-start = ((s32[32,32,1]{1,2,0:T(1,128)}), s32[32,32,1]{1,2,0:T(1,128)S(1)}, u32[]{:S(2)}, u32[]{:S(2)}) async-start(s32[32,32,1]{1,2,0:T(1,128)} %concatenate.137), calls=%async_computation | async-start | bytes 32768 | tf_op jit(solution)/shard_map/all_to_all | solution.py:94
  108.5 22.1 %collective-permute-start.4 = (f32[1,16,128]{2,0,1:T(1,128)S(1)}, f32[1,16,128]{2,0,1:T(1,128)S(1)}, u32[]{:S(2)}, u32[]{:S(2)}) collective-permute-start(f32[1,16,128]{2,0,1:T(1,128)S(1)} %bitcast.120), channel_id=1, source_target_pairs={{0,32},{32,64},{64,96},{96,128},{128,160},{160,192},{192,224},{224... | collective-permute-start | bytes 24584 | tf_op jit(solution)/shard_map/ppermute | solution.py:19
  110.7 19.9 %collective-permute-start.5 = (f32[1,16,128]{2,0,1:T(1,128)S(1)}, f32[1,16,128]{2,0,1:T(1,128)S(1)}, u32[]{:S(2)}, u32[]{:S(2)}) collective-permute-start(f32[1,16,128]{2,0,1:T(1,128)S(1)} %bitcast.119), channel_id=1, source_target_pairs={{32,0},{64,32},{96,64},{128,96},{160,128},{192,160},{224,192},{0,2... | collective-permute-start | bytes 24584 | tf_op jit(solution)/shard_map/ppermute | solution.py:22
  130.6 6.1 %collective-permute-start.6 = (f32[34,1,128]{2,0,1:T(8,128)S(1)}, f32[34,1,128]{2,0,1:T(8,128)S(1)}, u32[]{:S(2)}, u32[]{:S(2)}) collective-permute-start(f32[34,1,128]{2,0,1:T(8,128)S(1)} %get-tuple-element.68), channel_id=1, source_target_pairs={{0,1},{1,2},{2,3},{3,4},{4,5},{5,6},{6,7},{7,8},{8,9},{9,10},{10,1... | collective-permute-start | bytes 52232 | tf_op jit(solution)/shard_map/ppermute | solution.py:19
  131.7 5.0 %collective-permute-start.7 = (f32[34,1,128]{2,0,1:T(8,128)S(1)}, f32[34,1,128]{2,0,1:T(8,128)S(1)}, u32[]{:S(2)}, u32[]{:S(2)}) collective-permute-start(f32[34,1,128]{2,0,1:T(8,128)S(1)} %get-tuple-element.69), channel_id=1, source_target_pairs={{1,0},{2,1},{3,2},{4,3},{5,4},{6,5},{7,6},{8,7},{9,8},{10,9},{11,1... | collective-permute-start | bytes 52232 | tf_op jit(solution)/shard_map/ppermute | solution.py:22
  294.6 18.8 %collective-permute-start.8 = (f32[3,1,16,128]{3,2,1,0:T(8,128)S(1)}, f32[3,1,16,128]{3,2,1,0:T(8,128)S(1)}, u32[]{:S(2)}, u32[]{:S(2)}) collective-permute-start(f32[3,1,16,128]{3,2,1,0:T(8,128)S(1)} %get-tuple-element.46), channel_id=1, source_target_pairs={{0,32},{32,64},{64,96},{96,128},{128,160},{160,192},{192,224},{224... | collective-permute-start | bytes 73736 | tf_op jit(solution)/shard_map/ppermute | solution.py:19
  312.4 4.5 %collective-permute-start.9 = (f32[3,1,16,128]{3,2,1,0:T(8,128)S(1)}, f32[3,1,16,128]{3,2,1,0:T(8,128)S(1)}, u32[]{:S(2)}, u32[]{:S(2)}) collective-permute-start(f32[3,1,16,128]{3,2,1,0:T(8,128)S(1)} %get-tuple-element.47), channel_id=1, source_target_pairs={{32,0},{64,32},{96,64},{128,96},{160,128},{192,160},{224,192},{0,2... | collective-permute-start | bytes 73736 | tf_op jit(solution)/shard_map/ppermute | solution.py:22
  317.0 6.4 %collective-permute-start.10 = (f32[3,34,1,128]{3,2,1,0:T(1,128)S(1)}, f32[3,34,1,128]{3,2,1,0:T(1,128)S(1)}, u32[]{:S(2)}, u32[]{:S(2)}) collective-permute-start(f32[3,34,1,128]{3,2,1,0:T(1,128)S(1)} %get-tuple-element.44), channel_id=1, source_target_pairs={{0,1},{1,2},{2,3},{3,4},{4,5},{5,6},{6,7},{7,8},{8,9},{9,10},{10,1... | collective-permute-start | bytes 156680 | tf_op jit(solution)/shard_map/ppermute | solution.py:19
  317.1 6.3 %collective-permute-start.11 = (f32[3,34,1,128]{3,2,1,0:T(1,128)S(1)}, f32[3,34,1,128]{3,2,1,0:T(1,128)S(1)}, u32[]{:S(2)}, u32[]{:S(2)}) collective-permute-start(f32[3,34,1,128]{3,2,1,0:T(1,128)S(1)} %get-tuple-element.45), channel_id=1, source_target_pairs={{1,0},{2,1},{3,2},{4,3},{5,4},{6,5},{7,6},{8,7},{9,8},{10,9},{11,1... | collective-permute-start | bytes 156680 | tf_op jit(solution)/shard_map/ppermute | solution.py:22
  325.0 2.0 collective-permute-start.12
  326.1 4.3 %collective-permute-start.13 = (f32[1,16,128]{2,0,1:T(1,128)S(1)}, f32[1,16,128]{2,0,1:T(1,128)S(1)}, u32[]{:S(2)}, u32[]{:S(2)}) collective-permute-start(f32[1,16,128]{2,0,1:T(1,128)S(1)} %get-tuple-element.73), channel_id=1, source_target_pairs={{32,0},{64,32},{96,64},{128,96},{160,128},{192,160},{224,192},{0,2... | collective-permute-start | bytes 24584 | tf_op jit(solution)/shard_map/ppermute | solution.py:22
  330.4 6.3 %collective-permute-start.14 = (f32[34,1,128]{2,0,1:T(8,128)S(1)}, f32[34,1,128]{2,0,1:T(8,128)S(1)}, u32[]{:S(2)}, u32[]{:S(2)}) collective-permute-start(f32[34,1,128]{2,0,1:T(8,128)S(1)} %get-tuple-element.66), channel_id=1, source_target_pairs={{0,1},{1,2},{2,3},{3,4},{4,5},{5,6},{6,7},{7,8},{8,9},{9,10},{10,1... | collective-permute-start | bytes 52232 | tf_op jit(solution)/shard_map/ppermute | solution.py:19
  330.5 6.2 %collective-permute-start.15 = (f32[34,1,128]{2,0,1:T(8,128)S(1)}, f32[34,1,128]{2,0,1:T(8,128)S(1)}, u32[]{:S(2)}, u32[]{:S(2)}) collective-permute-start(f32[34,1,128]{2,0,1:T(8,128)S(1)} %get-tuple-element.67), channel_id=1, source_target_pairs={{1,0},{2,1},{3,2},{4,3},{5,4},{6,5},{7,6},{8,7},{9,8},{10,9},{11,1... | collective-permute-start | bytes 52232 | tf_op jit(solution)/shard_map/ppermute | solution.py:22
  337.4 1.7 collective-permute-start.16
  338.3 4.3 %collective-permute-start.17 = (f32[1,16,128]{2,0,1:T(1,128)S(1)}, f32[1,16,128]{2,0,1:T(1,128)S(1)}, u32[]{:S(2)}, u32[]{:S(2)}) collective-permute-start(f32[1,16,128]{2,0,1:T(1,128)S(1)} %get-tuple-element.71), channel_id=1, source_target_pairs={{32,0},{64,32},{96,64},{128,96},{160,128},{192,160},{224,192},{0,2... | collective-permute-start | bytes 24584 | tf_op jit(solution)/shard_map/ppermute | solution.py:22
  342.6 6.4 %collective-permute-start.18 = (f32[34,1,128]{2,0,1:T(8,128)S(1)}, f32[34,1,128]{2,0,1:T(8,128)S(1)}, u32[]{:S(2)}, u32[]{:S(2)}) collective-permute-start(f32[34,1,128]{2,0,1:T(8,128)S(1)} %get-tuple-element.64), channel_id=1, source_target_pairs={{0,1},{1,2},{2,3},{3,4},{4,5},{5,6},{6,7},{7,8},{8,9},{9,10},{10,1... | collective-permute-start | bytes 52232 | tf_op jit(solution)/shard_map/ppermute | solution.py:19
  342.7 6.3 %collective-permute-start.19 = (f32[34,1,128]{2,0,1:T(8,128)S(1)}, f32[34,1,128]{2,0,1:T(8,128)S(1)}, u32[]{:S(2)}, u32[]{:S(2)}) collective-permute-start(f32[34,1,128]{2,0,1:T(8,128)S(1)} %get-tuple-element.65), channel_id=1, source_target_pairs={{1,0},{2,1},{3,2},{4,3},{5,4},{6,5},{7,6},{8,7},{9,8},{10,9},{11,1... | collective-permute-start | bytes 52232 | tf_op jit(solution)/shard_map/ppermute | solution.py:22
  (23 other events, 163.4 us)
Sparse Core Ops, SparseCore 0:
  100.7 71.3 all-gather.2
